TPU v7x, 32 devices: a whole 2x2x4 slice. The times are simulated.
32 devices in a mesh: row: 4 (over z), col: 8 (over y, x, core).
Axes of the slice: x: 2, y: 2, z: 4, core: 2. Of those that a mesh axis runs over, the one named last changes fastest.
Arguments:
- covariance: float32 [8192, 8192], P('row', 'col'), as said below
- self_block: bfloat16 [8192, 512], P(('row', 'col')), may hold values from -0.25 to 0.25
- wake_block: bfloat16 [16, 4, 128, 128], replicated, may hold values from -0.375 to 0.375
- upstream: int32 [16, 4], replicated, may hold values from -1 to 15, as said below
- process_noise: float32 [8192], P('col'), may hold values from 0.5 to 2
- sensor_turbine: int32 [384], replicated, may hold values from 0 to 15
- azimuth_index: int32 [16], replicated, may hold values from 0 to 71
- sensor_weight: float32 [384, 512], replicated, may hold values from -0.25 to 0.25
- sensor_noise: float32 [384], replicated, may hold values from 0.5 to 2
Outputs:
- posterior: float32 [8192, 8192], P('row', 'col')
- kalman_gain: float32 [8192, 384], P('row', 'col')
Inputs may be any that keep to these rules, and one draw needn't show every extreme that they name: Row t lists distinct turbines other than t that lie upstream of t, valid entries first, then -1; some turbine lists 4. `covariance`: symmetric and positive definite.
All inputs are finite; a program needn't handle non-finite values.
Results may differ from a plain program's by a relative error of at most 0.0048.
Values may be sent and summed in bfloat16 or wider, within the bound.
No kernel may reach another device: no remote copies, remote signals or barrier semaphores. Data moves between devices by JAX's collectives and lax.ppermute only.
A program may use at most 128 MiB of HBM per device.

v0:
```python
import math
import jax
import jax.numpy as jnp
from jax import lax
from jax.sharding import PartitionSpec as P

TURB = 16
SPT = 512
INF = 128
NUP = 4
NAZ = 72


def broadcast(value, axis, root):
    mine = lax.axis_index(axis) == root
    return lax.psum(jnp.where(mine, value, jnp.zeros_like(value)), axis)


def observe_columns(sensor_weight, sensor_turbine, azimuth_index, start, count):
    sensors = sensor_weight.shape[0]
    matches = sensor_turbine[:, None] == jnp.arange(TURB)[None, :]
    rotor_index = jnp.sum(jnp.where(matches, azimuth_index[None, :], 0), axis=1)
    sensor_index = jnp.arange(sensors)
    blade_angle = rotor_index.astype(jnp.float32) * jnp.float32(2.0 * math.pi / NAZ) + (
        sensor_index % 3
    ).astype(jnp.float32) * jnp.float32(2.0 * math.pi / 3.0)
    positions = start + jnp.arange(count)
    turbine_of = positions // SPT
    offset_of = positions % SPT
    widened = jnp.tile(sensor_weight, (1, max(1, count // SPT)))
    weights = lax.dynamic_slice_in_dim(widened, start % SPT, count, 1)
    cosine = jnp.cos(blade_angle)[:, None]
    sine = jnp.sin(blade_angle)[:, None]
    factor = jnp.where(
        offset_of[None, :] < 2 * INF,
        jnp.float32(1.0),
        jnp.where(offset_of[None, :] < 3 * INF, cosine, sine),
    )
    return jnp.where(
        sensor_turbine[:, None] == turbine_of[None, :], weights * factor, jnp.float32(0.0)
    )


def split_bf16(x):
    high = x.astype(jnp.bfloat16)
    low = (x - high.astype(jnp.float32)).astype(jnp.bfloat16)
    return (high, low)


def coupling_matrix(wake_block, upstream, turbine):
    slots = upstream[turbine]
    blocks = jnp.zeros((INF, TURB, INF), jnp.bfloat16)
    for slot_index in range(NUP):
        anchor = slots[slot_index]
        hit = (jnp.arange(TURB) == anchor)[None, :, None]
        blocks = blocks + jnp.where(
            hit, wake_block[turbine, slot_index][:, None, :], jnp.zeros((), jnp.bfloat16)
        )
    return blocks.reshape(INF, TURB * INF)


def dot_f32(a, b, dims):
    return lax.dot_general(a, b, (dims, ((), ())), preferred_element_type=jnp.float32)


def shards(
    covariance,
    self_block,
    wake_block,
    upstream,
    process_noise,
    sensor_turbine,
    azimuth_index,
    sensor_weight,
    sensor_noise,
):
    row_count, col_count = covariance.shape
    row_start = lax.axis_index("row") * row_count
    col_start = lax.axis_index("col") * col_count
    per_row = row_count // SPT
    per_col = max(1, col_count // SPT)
    first_turbine = lax.axis_index("row") * per_row
    cov3 = covariance.reshape(per_row, SPT, col_count)
    inflow_all = lax.all_gather(cov3[:, :INF, :], "row", axis=0, tiled=True)
    inflow_high, inflow_low = split_bf16(inflow_all.reshape(TURB * INF, col_count))
    own_rows = lax.all_gather(self_block, "col", axis=0, tiled=True)
    cov_high, cov_low = split_bf16(cov3)
    blocks = []
    for local in range(per_row):
        turbine = first_turbine + local
        diag_rows = own_rows[local * SPT : (local + 1) * SPT]
        result = dot_f32(diag_rows, cov_high[local], ((1,), (0,))) + dot_f32(
            diag_rows, cov_low[local], ((1,), (0,))
        )
        coupling = coupling_matrix(wake_block, upstream, turbine)
        inflow_sum = dot_f32(coupling, inflow_high, ((1,), (0,))) + dot_f32(
            coupling, inflow_low, ((1,), (0,))
        )
        result = jnp.concatenate([result[:INF] + inflow_sum, result[INF:]], 0)
        blocks.append(result.astype(jnp.bfloat16))
    half_product = jnp.concatenate(blocks, 0)
    if col_count >= SPT:
        half3 = half_product.reshape(row_count, per_col, SPT)
        half_inflow = jnp.transpose(half3[:, :, :INF], (1, 0, 2))
        half_inflow_all = lax.all_gather(half_inflow, "col", axis=0, tiled=True)
        turbine_cols = [half3[:, local, :] for local in range(per_col)]
    else:
        full = lax.all_gather(half_product, "col", axis=1, tiled=True)
        half_inflow_all = jnp.transpose(full.reshape(row_count, TURB, SPT)[:, :, :INF], (1, 0, 2))
        turbine_cols = [lax.dynamic_slice_in_dim(full, col_start // SPT * SPT, SPT, 1)]
    target_rows = lax.dynamic_slice_in_dim(own_rows, col_start % row_count, col_count, 0)
    target_rows = broadcast(target_rows, "row", col_start // row_count)
    piece_width = min(col_count, SPT)
    pieces = []
    for local in range(per_col):
        turbine = col_start // SPT + local
        diag_rows = target_rows[local * piece_width : (local + 1) * piece_width]
        result = dot_f32(turbine_cols[local], diag_rows, ((1,), (1,)))
        coupling = coupling_matrix(wake_block, upstream, turbine).reshape(INF, TURB, INF)
        inflow_sum = dot_f32(half_inflow_all, coupling, ((0, 2), (1, 2)))
        inflow_sum = jnp.where(col_start % SPT == 0, inflow_sum, jnp.float32(0.0))
        pieces.append(jnp.concatenate([result[:, :INF] + inflow_sum, result[:, INF:]], 1))
    predicted = jnp.concatenate(pieces, 1)
    row_ids = row_start + jnp.arange(row_count)
    col_ids = col_start + jnp.arange(col_count)
    predicted = predicted + jnp.where(
        row_ids[:, None] == col_ids[None, :], process_noise[None, :], jnp.float32(0.0)
    )
    col_observe = observe_columns(
        sensor_weight, sensor_turbine, azimuth_index, col_start, col_count
    )
    partial_cross = jnp.dot(predicted, col_observe.T, precision=lax.Precision.HIGHEST)
    cross_cov = lax.psum(partial_cross, "col")
    row_observe = observe_columns(
        sensor_weight, sensor_turbine, azimuth_index, row_start, row_count
    )
    partial_innovation = jnp.dot(row_observe, cross_cov, precision=lax.Precision.HIGHEST)
    innovation = lax.psum(partial_innovation, "row") + jnp.diag(sensor_noise)
    symmetric = 0.5 * (innovation + innovation.T)
    lower = jnp.linalg.cholesky(symmetric)
    sensors = symmetric.shape[0]
    lower_inverse = jax.scipy.linalg.solve_triangular(
        lower, jnp.eye(sensors, dtype=jnp.float32), lower=True
    )
    inverse = jnp.dot(lower_inverse.T, lower_inverse, precision=lax.Precision.HIGHEST)
    gain_block = jnp.dot(cross_cov, inverse, precision=lax.Precision.HIGHEST)
    target_cross = lax.dynamic_slice_in_dim(cross_cov, col_start % row_count, col_count, 0)
    target_cross = broadcast(target_cross, "row", col_start // row_count)
    posterior = predicted - jnp.dot(gain_block, target_cross.T, precision=lax.Precision.HIGHEST)
    share = gain_block.shape[1] // lax.axis_size("col")
    gain_share = lax.dynamic_slice_in_dim(gain_block, lax.axis_index("col") * share, share, 1)
    return (posterior, gain_share)


def solution(mesh):
    in_specs = (P("row", "col"), P(("row", "col"), None), P(), P(), P("col"), P(), P(), P(), P())
    out_specs = (P("row", "col"), P("row", "col"))
    return jax.shard_map(shards, mesh=mesh, in_specs=in_specs, out_specs=out_specs, check_vma=False)
```

profile of v0, /device:TPU:0, one launch (start us, length us, event | category | flops | bytes accessed | tf_op | source)
XLA Modules:
  0.0 682.4 jit_solution(16363561873510141729)
XLA Ops:
  8.0 3.1 slice.340
  32.1 11.9 %subtract_convert_fusion.1 = (bf16[4,512,1024]{2,1,0:T(8,128)(2,1)}, bf16[4,512,1024]{2,1,0:T(8,128)(2,1)}) fusion(f32[4,512,1024]{2,1,0:T(8,128)} %bitcast.250), kind=kLoop, calls=%fused_computation.4 | loop fusion | flops 8388608 | bytes 16777216 | tf_op jit(solution)/shard_map/convert_element_type | solution.py:46
  44.0 2.1 fusion.39
  46.1 2.3 bitcast_add_fusion.1
  62.0 129.8 %all-gather.6.cloned.1.call-done = f32[16,128,1024]{2,1,0:T(8,128)} async-done(((f32[4,128,1024]{2,1,0:T(8,128)}), f32[16,128,1024]{2,1,0:T(8,128)}) %all-gather.6.cloned.1.call-update) | async-done | bytes 8388624 | tf_op jit(solution)/shard_map/all_gather | solution.py:84
  191.8 8.7 %subtract_convert_fusion = (bf16[16,128,1024]{2,1,0:T(8,128)(2,1)S(1)}, bf16[16,128,1024]{2,1,0:T(8,128)(2,1)S(1)}) fusion(f32[16,128,1024]{2,1,0:T(8,128)} %all-gather.6.cloned.1.call-done), kind=kLoop, calls=%fused_computation.3 | loop fusion | flops 8388608 | bytes 16777216 | tf_op jit(solution)/shard_map/convert_element_type | solution.py:46
  212.3 2.0 copy-done.4
  223.4 20.8 %all-reduce.6.cloned.1.call-done = bf16[1024,512]{1,0:T(8,128)(2,1)} async-done(((bf16[1024,512]{1,0:T(8,128)(2,1)}), bf16[1024,512]{1,0:T(8,128)(2,1)}) %all-reduce.6.cloned.1.call-update) | async-done | bytes 1048592 | tf_op jit(solution)/shard_map/psum | solution.py:16
  244.2 3.0 fusion.10
  247.4 3.5 copy-done.5
  252.5 2.0 copy-done.1
  256.4 43.6 %all-gather.8.cloned.1.call-done = bf16[16,2048,128]{2,1,0:T(8,128)(2,1)} async-done(((bf16[2,2048,128]{2,1,0:T(8,128)(2,1)}), bf16[16,2048,128]{2,1,0:T(8,128)(2,1)}) %all-gather.8.cloned.1.call-update) | async-done | bytes 8388624 | tf_op jit(solution)/shard_map/all_gather | solution.py:105
  299.9 6.6 fusion.9
  306.6 4.5 fusion.8
  312.1 38.5 %fusion.17 = f32[2048,384]{1,0:T(8,128)} fusion(f32[384,1024]{1,0:T(8,128)S(1)} %bitcast.258, f32[384]{0:T(512)S(1)} %get-tuple-element.103, f32[384]{0:T(512)S(1)} %get-tuple-element.102, s32[1024]{0:T(1024)S(1)} %get-tuple-element.104, s32[384]{0:T(512)S(1)} %copy-done.33, pred[1024]{0:T(1024)(128)(4,1)S(1)} %get-tuple-element.106, ...), kind=kOutput, calls=%fused_computation.36 | convolution fusion | flops 9678225408 | bytes 13134336 | tf_op jit(solution)/shard_map/dot_general | solution.py:132
  353.8 66.4 %all-reduce.8.cloned.1.call-done = f32[2048,384]{1,0:T(8,128)} async-done(((f32[2048,384]{1,0:T(8,128)}), f32[2048,384]{1,0:T(8,128)}) %all-reduce.8.cloned.1.call-update) | async-done | bytes 3145744 | tf_op jit(solution)/shard_map/psum | solution.py:133
  420.2 2.7 dynamic-slice_select_fusion
  422.8 8.5 %fusion = f32[384,384]{0,1:T(8,128)} fusion(f32[2048,384]{1,0:T(8,128)} %all-reduce.8.cloned.1.call-done, f32[384,2048]{1,0:T(8,128)S(1)} %bitcast.253, f32[384]{0:T(512)S(1)} %get-tuple-element.103, f32[384]{0:T(512)S(1)} %get-tuple-element.102, s32[2048]{0:T(1024)S(1)} %add_select_fusion.1, s32[384]{0:T(512)S(1)} %copy-done.33, ...), kind=kOutput, calls=%fused_computation.6 | convolution fusion | flops 3627810816 | bytes 6898176 | tf_op jit(solution)/shard_map/dot_general | solution.py:137
  432.8 88.4 %all-reduce.10.cloned.1.call-done = (f32[384,384]{0,1:T(8,128)}, f32[1024,384]{1,0:T(8,128)}) async-done(((f32[384,384]{0,1:T(8,128)}, f32[1024,384]{1,0:T(8,128)}), (f32[384,384]{0,1:T(8,128)}, f32[1024,384]{1,0:T(8,128)})) %all-reduce.10.cloned.1.call-update) | async-done | bytes 2162704 | tf_op jit(solution)/shard_map/psum | solution.py:138
  524.0 11.8 %cholesky.76 = f32[128,128]{1,0:T(8,128)S(1)} custom-call(f32[128,128]{1,0:T(8,128)S(1)} %cholesky.189), custom_call_target="Cholesky" | custom-call | tf_op jit(solution)/shard_map/jit(cholesky)/cholesky | solution.py:140
  536.6 9.8 %custom-call.23 = f32[1,128,128]{1,2,0:T(8,128)S(1)} custom-call(f32[1,128,128]{2,1,0:T(8,128)S(1)} %get-tuple-element.71), custom_call_target="InvertDiagBlocksLowerTriangular" | custom-call | tf_op jit(solution)/shard_map/jit(cholesky)/cholesky | solution.py:140
  547.1 11.7 %cholesky.160 = f32[128,128]{1,0:T(8,128)S(1)} custom-call(f32[128,128]{1,0:T(8,128)S(1)} %cholesky.193), custom_call_target="Cholesky" | custom-call | tf_op jit(solution)/shard_map/jit(cholesky)/cholesky | solution.py:140
  560.1 10.4 %custom-call.24 = f32[1,128,128]{1,2,0:T(8,128)} custom-call(f32[1,128,128]{2,1,0:T(8,128)S(1)} %get-tuple-element.69), custom_call_target="InvertDiagBlocksLowerTriangular" | custom-call | tf_op jit(solution)/shard_map/jit(cholesky)/cholesky | solution.py:140
  574.8 11.9 %cholesky.179 = f32[128,128]{1,0:T(8,128)S(1)} custom-call(f32[128,128]{1,0:T(8,128)S(1)} %convolution_subtract_fusion.4), custom_call_target="Cholesky" | custom-call | tf_op jit(solution)/shard_map/jit(cholesky)/cholesky | solution.py:140
  595.3 11.1 %while.1 = (s32[]{:T(128)}, f32[384,384]{0,1:T(8,128)}, s32[3,2]{0,1:T(2,128)S(1)}, f32[3,128,128]{2,1,0:T(8,128)}, s32[]{:T(128)}) while((s32[]{:T(128)}, f32[384,384]{0,1:T(8,128)}, s32[3,2]{0,1:T(2,128)S(1)}, f32[3,128,128]{2,1,0:T(8,128)}, s32[]{:T(128)}) %tuple.95), condition=%wide.while_cond, body=%wide.while_body.sunk | while | flops 2 | bytes 393329 | solution.py:142
  596.0 2.3 dynamic-slice.7
  599.7 2.3 dynamic-slice.7
  603.4 2.3 dynamic-slice.7
  606.4 30.3 %custom-call.25 = f32[3,128,128]{1,2,0:T(8,128)S(1)} custom-call(f32[3,128,128]{2,1,0:T(8,128)} %get-tuple-element.9), custom_call_target="InvertDiagBlocksLowerTriangular" | custom-call | tf_op jit(solution)/shard_map/jit(_solve_triangular)/triangular_solve | solution.py:142
  642.8 5.4 fusion.158
  648.3 16.8 %convolution_subtract_fusion = f32[2048,1024]{0,1:T(8,128)} fusion(f32[2048,384]{0,1:T(8,128)S(1)} %fusion.158, f32[1024,384]{1,0:T(8,128)S(1)} %copy-done.36, f32[1024]{0:T(1024)S(1)} %copy-done.38, s32[1024]{0:T(1024)S(1)} %copy-done.32, s32[2048]{0:T(1024)S(1)} %copy-done.29, f32[2048,384]{0,1:T(8,128)S(1)} %copy-done.12, f32[2048,128]{0,1:T(8,128)S(1)} %copy-done.56, ...), kind=kOutput, calls=%fused_computation.5 | convolution fusion | flops 9678356480 | bytes 21512192 | tf_op jit(solution)/shard_map/dot_general | solution.py:149
  665.9 9.2 %copy.81 = f32[2048,1024]{1,0:T(8,128)} copy(f32[2048,1024]{0,1:T(8,128)} %convolution_subtract_fusion) | data formatting | bytes 16777216
  (245 shorter events, 91.9 us)
Async XLA Ops:
  7.2 36.8 %all-gather.4.cloned.1.call-start = ((), (), s32[]{:S(2)}) async-start(), calls=%async_computation | async-start | bytes 2359296 | tf_op jit(solution)/shard_map/all_gather | solution.py:86
  7.9 183.8 %all-gather.6.cloned.1.call-start = ((), (), s32[]{:S(2)}) async-start(), calls=%async_computation.1 | async-start | bytes 10485760 | tf_op jit(solution)/shard_map/all_gather | solution.py:84
  11.1 233.1 %all-reduce.6.cloned.1.call-start = ((), (), s32[]{:S(2)}) async-start(), calls=%async_computation.2 | async-start | bytes 2097152 | tf_op jit(solution)/shard_map/psum | solution.py:16
  46.1 6.2 copy-start.3
  61.7 238.3 %all-gather.8.cloned.1.call-start = ((), (), s32[]{:S(2)}) async-start(), calls=%async_computation.3 | async-start | bytes 9437184 | tf_op jit(solution)/shard_map/all_gather | solution.py:105
  191.8 8.8 %copy-start.24 = (bf16[128,128]{1,0:T(8,128)(2,1)S(1)}, bf16[128,128]{1,0:T(8,128)(2,1)}, u32[]{:S(2)}) copy-start(bf16[128,128]{1,0:T(8,128)(2,1)} %get-tuple-element.54) | copy-start | bytes 98308
  191.8 8.8 %copy-start.25 = (bf16[128,128]{1,0:T(8,128)(2,1)S(1)}, bf16[128,128]{1,0:T(8,128)(2,1)}, u32[]{:S(2)}) copy-start(bf16[128,128]{1,0:T(8,128)(2,1)} %get-tuple-element.55) | copy-start | bytes 98308
  191.8 8.8 %copy-start.26 = (bf16[128,128]{1,0:T(8,128)(2,1)S(1)}, bf16[128,128]{1,0:T(8,128)(2,1)}, u32[]{:S(2)}) copy-start(bf16[128,128]{1,0:T(8,128)(2,1)} %get-tuple-element.56) | copy-start | bytes 98308
  191.8 8.8 %copy-start.27 = (bf16[128,128]{1,0:T(8,128)(2,1)S(1)}, bf16[128,128]{1,0:T(8,128)(2,1)}, u32[]{:S(2)}) copy-start(bf16[128,128]{1,0:T(8,128)(2,1)} %get-tuple-element.57) | copy-start | bytes 98308
  214.3 8.9 %copy-start.33 = (s32[384]{0:T(512)S(1)}, s32[384]{0:T(512)}, u32[]{:S(2)}) copy-start(s32[384]{0:T(512)} %param.14) | copy-start | bytes 4612
  214.3 8.9 %copy-start.34 = (s32[16]{0:T(128)S(1)}, s32[16]{0:T(128)}, u32[]{:S(2)}) copy-start(s32[16]{0:T(128)} %param.15) | copy-start | bytes 196
  215.5 204.7 %all-reduce.8.cloned.1.call-start = ((), (), s32[]{:S(2)}) async-start(), calls=%async_computation.4 | async-start | bytes 6291456 | tf_op jit(solution)/shard_map/psum | solution.py:133
  223.2 87.9 %copy-start.31 = (s32[1024]{0:T(1024)}, s32[1024]{0:T(1024)S(1)}, u32[]{:S(2)}) copy-start(s32[1024]{0:T(1024)S(1)} %get-tuple-element.105) | copy-start | bytes 12292
  223.3 87.9 %copy-start.28 = (s32[2048]{0:T(1024)}, s32[2048]{0:T(1024)S(1)}, u32[]{:S(2)}) copy-start(s32[2048]{0:T(1024)S(1)} %iota_add_fusion) | copy-start | bytes 24580
  247.2 5.3 copy-start
  251.2 59.9 %copy-start.11 = (f32[2048,384]{0,1:T(8,128)}, f32[2048,384]{0,1:T(8,128)S(1)}, u32[]{:S(2)}) copy-start(f32[2048,384]{0,1:T(8,128)S(1)} %slice.365) | copy-start | bytes 9437188
  299.9 6.6 copy-start.35
  306.6 5.5 copy-start.13
  306.6 5.5 copy-start.21
  306.6 5.5 copy-start.37
  350.6 170.6 %all-reduce.10.cloned.1.call-start = ((), (), s32[]{:S(2)}) async-start(), calls=%async_computation.5 | async-start | bytes 4325376 | tf_op jit(solution)/shard_map/psum | solution.py:138
  422.8 98.4 %copy-start.30 = (f32[384]{0:T(512)S(1)}, f32[384]{0:T(512)}, u32[]{:S(2)}) copy-start(f32[384]{0:T(512)} %param.17) | copy-start | bytes 4612
  524.0 46.6 %copy-start.20 = (f32[384,384]{1,0:T(8,128)}, f32[384,384]{1,0:T(8,128)S(1)}, u32[]{:S(2)}) copy-start(f32[384,384]{1,0:T(8,128)S(1)} %fusion.56) | copy-start | bytes 1769476
  570.6 72.2 %copy-start.7 = (f32[2048,384]{1,0:T(8,128)S(1)}, f32[2048,384]{1,0:T(8,128)}, u32[]{:S(2)}) copy-start(f32[2048,384]{1,0:T(8,128)} %all-reduce.8.cloned.1.call-done) | copy-start | bytes 9437188
  637.0 11.1 %copy-start.56 = (f32[2048,128]{0,1:T(8,128)S(1)}, f32[2048,128]{0,1:T(8,128)}, u32[]{:S(2)}) copy-start(f32[2048,128]{0,1:T(8,128)} %copy-done.55) | copy-start | bytes 3145732
  639.0 9.2 %copy-start.54 = (f32[2048,128]{0,1:T(8,128)S(1)}, f32[2048,128]{0,1:T(8,128)}, u32[]{:S(2)}) copy-start(f32[2048,128]{0,1:T(8,128)} %copy-done.53) | copy-start | bytes 3145732
  640.9 7.3 %copy-start.12 = (f32[2048,384]{0,1:T(8,128)S(1)}, f32[2048,384]{0,1:T(8,128)}, u32[]{:S(2)}) copy-start(f32[2048,384]{0,1:T(8,128)} %copy-done.11) | copy-start | bytes 9437188
  640.9 7.3 %copy-start.14 = (f32[2048,384]{0,1:T(8,128)S(1)}, f32[2048,384]{0,1:T(8,128)}, u32[]{:S(2)}) copy-start(f32[2048,384]{0,1:T(8,128)} %slice.361) | copy-start | bytes 9437188
  640.9 7.3 %copy-start.29 = (s32[2048]{0:T(1024)S(1)}, s32[2048]{0:T(1024)}, u32[]{:S(2)}) copy-start(s32[2048]{0:T(1024)} %copy-done.28) | copy-start | bytes 24580
  640.9 7.3 %copy-start.32 = (s32[1024]{0:T(1024)S(1)}, s32[1024]{0:T(1024)}, u32[]{:S(2)}) copy-start(s32[1024]{0:T(1024)} %copy-done.31) | copy-start | bytes 12292
  640.9 7.3 %copy-start.36 = (f32[1024,384]{1,0:T(8,128)S(1)}, f32[1024,384]{1,0:T(8,128)}, u32[]{:S(2)}) copy-start(f32[1024,384]{1,0:T(8,128)} %get-tuple-element.37) | copy-start | bytes 4718596
  641.0 7.3 %copy-start.38 = (f32[1024]{0:T(1024)S(1)}, f32[1024]{0:T(1024)}, u32[]{:S(2)}) copy-start(f32[1024]{0:T(1024)} %param.13) | copy-start | bytes 12292
  (31 other events, 68.8 us)
Sparse Core Ops, SparseCore 0:
  9.9 30.5 all-gather.3
  42.1 149.6 all-gather.5
  194.1 50.0 all-reduce.5
  246.1 53.7 all-gather.7
  350.7 69.4 all-reduce.7
  431.5 89.6 all-reduce.9
where the time goes:
time: 690 us; the launch traced here: 682 us
  waiting for transfers between devices  350 us (51%)
  other arithmetic  144 us (21%)
  matrix products  112 us (16%)
  local copies, waits for them, and re-layouts  58.7 us (9%)
  between operations  17.8 us (3%)
    all_gather x1, waiting for transfers between devices, shards(): inflow_all = lax.all_gather(cov3[:, :INF, :], 'row', axis=0, tiled=True)  130 us
    psum x1, waiting for transfers between devices, shards(): innovation = lax.psum(partial_innovation, 'row') + jnp.diag(sensor_noise)  88.4 us
    psum x1, waiting for transfers between devices, shards(): cross_cov = lax.psum(partial_cross, 'col')  66.4 us
    another operation x11, other arithmetic, shards(): lower = jnp.linalg.cholesky(symmetric)  60.4 us
    all_gather x1, waiting for transfers between devices, shards(): half_inflow_all = lax.all_gather(half_inflow, 'col', axis=0, tiled=True)  43.6 us
    dot_general x1, matrix products, shards(): jnp.dot(predicted, col_observe.T, precision=lax.Precision.HIGHEST)  38.5 us
    dot_general x20, matrix products, dot_f32(): lax.dot_general(a, b, (dims, ((), ())), preferred_element_type=jnp.float32)  34.1 us
    another operation x3, other arithmetic, shards(): jax.scipy.linalg.solve_triangular(lower, jnp.eye(sensors, dtype=jnp.float...  32.7 us
  transfers between devices with their start and end apart: 6, of which 5 were waited for; matrix products, arithmetic and copies ran while one was open for 13% of the time, Pallas kernels for 0%

commit v1 on v0

--- a/solution.py
+++ b/solution.py
@@ -135,7 +135,7 @@
         sensor_weight, sensor_turbine, azimuth_index, row_start, row_count
     )
     partial_innovation = jnp.dot(row_observe, cross_cov, precision=lax.Precision.HIGHEST)
-    innovation = lax.psum(partial_innovation, "row") + jnp.diag(sensor_noise)
+    innovation = jnp.sum(lax.all_gather(partial_innovation, "row"), axis=0) + jnp.diag(sensor_noise)
     symmetric = 0.5 * (innovation + innovation.T)
     lower = jnp.linalg.cholesky(symmetric)
     sensors = symmetric.shape[0]

time: 690 us -> 647 us (0.938)
  waiting for transfers between devices: 350 us -> 308 us
    psum x1 -> x0, waiting for transfers between devices: 88.4 us -> none  [shards(): innovation = lax.psum(partial_innovation, 'row') + jnp.diag(sensor_noise)]
    all_gather x0 -> x1, waiting for transfers between devices: none -> 48 us  [shards(): lax.all_gather(partial_innovation, 'row')]
    dot_general x1, matrix products: 38.5 us -> 29.1 us  [shards(): jnp.dot(predicted, col_observe.T, precision=lax.Precision.HIGHEST)]
    unnamed x124 -> x114, local copies, waits for them, and re-layouts: 27.4 us -> 30.8 us
    psum x1 -> x2, waiting for transfers between devices: 20.8 us -> 20.8 us  [broadcast(): return lax.psum(jnp.where(mine, value, jnp.zeros_like(value)), axis)]
  transfers between devices with their start and end apart: 6 -> 7, of which waited for: 5 -> 5; matrix products, arithmetic and copies ran while one was open for 13% -> 34% of each run, Pallas kernels for 0% -> 0%
where the time goes in v1:
time: 647 us; the launch traced here: 640 us
  waiting for transfers between devices  308 us (48%)
  other arithmetic  143 us (22%)
  matrix products  110 us (17%)
  local copies, waits for them, and re-layouts  61.4 us (9%)
  between operations  17.3 us (3%)
    all_gather x1, waiting for transfers between devices, shards(): inflow_all = lax.all_gather(cov3[:, :INF, :], 'row', axis=0, tiled=True)  130 us
    psum x1, waiting for transfers between devices, shards(): cross_cov = lax.psum(partial_cross, 'col')  64.7 us
    another operation x11, other arithmetic, shards(): lower = jnp.linalg.cholesky(symmetric)  58.5 us
    all_gather x1, waiting for transfers between devices, shards(): lax.all_gather(partial_innovation, 'row')  48 us
    all_gather x1, waiting for transfers between devices, shards(): half_inflow_all = lax.all_gather(half_inflow, 'col', axis=0, tiled=True)  43.5 us
    dot_general x20, matrix products, dot_f32(): lax.dot_general(a, b, (dims, ((), ())), preferred_element_type=jnp.float32)  34 us
    another operation x3, other arithmetic, shards(): jax.scipy.linalg.solve_triangular(lower, jnp.eye(sensors, dtype=jnp.float...  33.4 us
    unnamed x114, local copies, waits for them, and re-layouts  30.8 us
  transfers between devices with their start and end apart: 7, of which 5 were waited for; matrix products, arithmetic and copies ran while one was open for 34% of the time, Pallas kernels for 0%

profile of v1, /device:TPU:0, one launch (start us, length us, event | category | flops | bytes accessed | tf_op | source)
XLA Modules:
  0.0 639.5 jit_solution(11074762497728134798)
XLA Ops:
  8.0 3.2 slice.340
  32.1 11.9 %subtract_convert_fusion.1 = (bf16[4,512,1024]{2,1,0:T(8,128)(2,1)}, bf16[4,512,1024]{2,1,0:T(8,128)(2,1)}) fusion(f32[4,512,1024]{2,1,0:T(8,128)} %bitcast.246), kind=kLoop, calls=%fused_computation.4 | loop fusion | flops 8388608 | bytes 16777216 | tf_op jit(solution)/shard_map/convert_element_type | solution.py:46
  44.0 2.1 fusion.39
  46.2 2.3 bitcast_add_fusion.1
  61.9 129.9 %all-gather.8.cloned.1.call-done = f32[16,128,1024]{2,1,0:T(8,128)} async-done(((f32[4,128,1024]{2,1,0:T(8,128)}), f32[16,128,1024]{2,1,0:T(8,128)}) %all-gather.8.cloned.1.call-update) | async-done | bytes 8388624 | tf_op jit(solution)/shard_map/all_gather | solution.py:84
  191.8 8.6 %subtract_convert_fusion = (bf16[16,128,1024]{2,1,0:T(8,128)(2,1)S(1)}, bf16[16,128,1024]{2,1,0:T(8,128)(2,1)S(1)}) fusion(f32[16,128,1024]{2,1,0:T(8,128)} %all-gather.8.cloned.1.call-done), kind=kLoop, calls=%fused_computation.3 | loop fusion | flops 8388608 | bytes 16777216 | tf_op jit(solution)/shard_map/convert_element_type | solution.py:46
  223.5 20.8 %all-reduce.5.cloned.1.call-done = bf16[1024,512]{1,0:T(8,128)(2,1)} async-done(((bf16[1024,512]{1,0:T(8,128)(2,1)}), bf16[1024,512]{1,0:T(8,128)(2,1)}) %all-reduce.5.cloned.1.call-update) | async-done | bytes 1048592 | tf_op jit(solution)/shard_map/psum | solution.py:16
  244.3 3.0 fusion.10
  247.5 3.5 copy-done.5
  256.4 43.5 %all-gather.10.cloned.1.call-done = bf16[16,2048,128]{2,1,0:T(8,128)(2,1)} async-done(((bf16[2,2048,128]{2,1,0:T(8,128)(2,1)}), bf16[16,2048,128]{2,1,0:T(8,128)(2,1)}) %all-gather.10.cloned.1.call-update) | async-done | bytes 8388624 | tf_op jit(solution)/shard_map/all_gather | solution.py:105
  299.9 6.6 %fusion.9 = f32[2048,128]{0,1:T(8,128)S(1)} fusion(bf16[16,2048,128]{2,1,0:T(8,128)(2,1)} %all-gather.10.cloned.1.call-done, f32[2048,512]{0,1:T(8,128)} %copy-done.1, pred[16]{0:T(512)(128)(4,1)S(1)} %iota_compare_fusion.10, pred[16]{0:T(512)(128)(4,1)S(1)} %iota_compare_fusion.11, pred[16]{0:T(512)(128)(4,1)S(1)} %iota_compare_fusion.12, ...), kind=kOutput, calls=%fused_computation.17 | convolution fusion | flops 1076101120 | bytes 10616897 | tf_op jit(solution)/shard_map/dot_general | solution.py:63
  306.6 4.5 fusion.8
  312.1 29.1 %fusion.17 = f32[2048,384]{1,0:T(8,128)} fusion(f32[384,1024]{1,0:T(8,128)S(1)} %bitcast.256, f32[384]{0:T(512)S(1)} %get-tuple-element.92, f32[384]{0:T(512)S(1)} %get-tuple-element.91, s32[1024]{0:T(1024)S(1)} %get-tuple-element.95, s32[384]{0:T(512)S(1)} %copy-done.31, pred[1024]{0:T(1024)(128)(4,1)S(1)} %get-tuple-element.97, ...), kind=kOutput, calls=%fused_computation.36 | convolution fusion | flops 9678225408 | bytes 13134336 | tf_op jit(solution)/shard_map/dot_general | solution.py:132
  343.0 3.1 copy.70
  346.1 64.7 %all-reduce.7.cloned.1.call-done = f32[2048,384]{1,0:T(8,128)} async-done(((f32[2048,384]{1,0:T(8,128)}), f32[2048,384]{1,0:T(8,128)}) %all-reduce.7.cloned.1.call-update) | async-done | bytes 3145744 | tf_op jit(solution)/shard_map/psum | solution.py:133
  410.8 9.4 %fusion = f32[384,384]{1,0:T(8,128)} fusion(f32[2048,384]{1,0:T(8,128)} %all-reduce.7.cloned.1.call-done, f32[384,2048]{1,0:T(8,128)} %bitcast.250, f32[384]{0:T(512)S(1)} %get-tuple-element.92, f32[384]{0:T(512)S(1)} %get-tuple-element.91, s32[2048]{0:T(1024)S(1)} %add_select_fusion.1, s32[384]{0:T(512)S(1)} %copy-done.31, ...), kind=kOutput, calls=%fused_computation.6 | convolution fusion | flops 3627810816 | bytes 6898176 | tf_op jit(solution)/shard_map/dot_general | solution.py:137
  423.0 48.0 %all-gather.12.cloned.1.call-done = f32[1536,384]{1,0:T(8,128)} async-done(((f32[384,384]{1,0:T(8,128)}), f32[1536,384]{1,0:T(8,128)}) %all-gather.12.cloned.1.call-update) | async-done | bytes 2359312 | tf_op jit(solution)/shard_map/all_gather | solution.py:138
  470.9 2.7 reduce_sum.25
  473.6 2.1 copy.53
  477.9 11.7 %cholesky.76 = f32[128,128]{1,0:T(8,128)S(1)} custom-call(f32[128,128]{1,0:T(8,128)S(1)} %cholesky.189), custom_call_target="Cholesky" | custom-call | tf_op jit(solution)/shard_map/jit(cholesky)/cholesky | solution.py:140
  491.2 9.8 %custom-call.23 = f32[1,128,128]{1,2,0:T(8,128)S(1)} custom-call(f32[1,128,128]{2,1,0:T(8,128)S(1)} %get-tuple-element.60), custom_call_target="InvertDiagBlocksLowerTriangular" | custom-call | tf_op jit(solution)/shard_map/jit(cholesky)/cholesky | solution.py:140
  504.1 11.7 %cholesky.160 = f32[128,128]{1,0:T(8,128)S(1)} custom-call(f32[128,128]{1,0:T(8,128)S(1)} %cholesky.193), custom_call_target="Cholesky" | custom-call | tf_op jit(solution)/shard_map/jit(cholesky)/cholesky | solution.py:140
  517.1 10.2 %custom-call.24 = f32[1,128,128]{1,2,0:T(8,128)S(1)} custom-call(f32[1,128,128]{2,1,0:T(8,128)S(1)} %get-tuple-element.57), custom_call_target="InvertDiagBlocksLowerTriangular" | custom-call | tf_op jit(solution)/shard_map/jit(cholesky)/cholesky | solution.py:140
  529.4 11.7 %cholesky.179 = f32[128,128]{1,0:T(8,128)S(1)} custom-call(f32[128,128]{1,0:T(8,128)S(1)} %convolution_subtract_fusion.4), custom_call_target="Cholesky" | custom-call | tf_op jit(solution)/shard_map/jit(cholesky)/cholesky | solution.py:140
  546.9 10.6 %while.1 = (s32[]{:T(128)}, f32[384,384]{1,0:T(8,128)}, s32[3,2]{0,1:T(2,128)S(1)}, f32[3,128,128]{2,1,0:T(8,128)}, s32[]{:T(128)}) while((s32[]{:T(128)}, f32[384,384]{1,0:T(8,128)}, s32[3,2]{0,1:T(2,128)S(1)}, f32[3,128,128]{2,1,0:T(8,128)}, s32[]{:T(128)}) %tuple.95), condition=%wide.while_cond, body=%wide.while_body.sunk | while | flops 2 | bytes 132205 | solution.py:142
  547.5 2.9 bitcast_dynamic-update-slice_fusion.10
  551.1 2.9 bitcast_dynamic-update-slice_fusion.10
  554.6 2.8 bitcast_dynamic-update-slice_fusion.10
  557.4 30.9 %custom-call.25 = f32[3,128,128]{1,2,0:T(8,128)} custom-call(f32[3,128,128]{2,1,0:T(8,128)} %get-tuple-element.9), custom_call_target="InvertDiagBlocksLowerTriangular" | custom-call | tf_op jit(solution)/shard_map/jit(_solve_triangular)/triangular_solve | solution.py:142
  596.0 5.4 fusion.156
  603.9 19.4 %convolution_subtract_fusion = f32[2048,1024]{0,1:T(8,128)} fusion(f32[2048,384]{0,1:T(8,128)} %copy-done.8, f32[1024,384]{1,0:T(8,128)} %all-reduce.9.cloned.1.call-done, f32[1024]{0:T(1024)S(1)} %copy-done.35, s32[1024]{0:T(1024)S(1)} %copy-done.30, s32[2048]{0:T(1024)S(1)} %copy-done.28, f32[2048,384]{0,1:T(8,128)} %copy-done.12, ...), kind=kOutput, calls=%fused_computation.5 | convolution fusion | flops 9678356480 | bytes 21512192 | tf_op jit(solution)/shard_map/dot_general | solution.py:149
  623.2 9.2 %copy.55 = f32[2048,1024]{1,0:T(8,128)} copy(f32[2048,1024]{0,1:T(8,128)} %convolution_subtract_fusion) | data formatting | bytes 16777216
  (223 shorter events, 94.7 us)
Async XLA Ops:
  7.2 4.1 copy-start.21
  7.2 36.9 %all-gather.6.cloned.1.call-start = ((), (), s32[]{:S(2)}) async-start(), calls=%async_computation | async-start | bytes 2359296 | tf_op jit(solution)/shard_map/all_gather | solution.py:86
  7.9 183.8 %all-gather.8.cloned.1.call-start = ((), (), s32[]{:S(2)}) async-start(), calls=%async_computation.1 | async-start | bytes 10485760 | tf_op jit(solution)/shard_map/all_gather | solution.py:84
  11.1 233.1 %all-reduce.5.cloned.1.call-start = ((), (), s32[]{:S(2)}) async-start(), calls=%async_computation.2 | async-start | bytes 2097152 | tf_op jit(solution)/shard_map/psum | solution.py:16
  46.2 4.4 copy-start.6
  46.2 6.2 copy-start.3
  61.7 238.3 %all-gather.10.cloned.1.call-start = ((), (), s32[]{:S(2)}) async-start(), calls=%async_computation.3 | async-start | bytes 9437184 | tf_op jit(solution)/shard_map/all_gather | solution.py:105
  191.8 8.7 %copy-start.22 = (bf16[128,128]{1,0:T(8,128)(2,1)S(1)}, bf16[128,128]{1,0:T(8,128)(2,1)}, u32[]{:S(2)}) copy-start(bf16[128,128]{1,0:T(8,128)(2,1)} %get-tuple-element.40) | copy-start | bytes 98308
  191.8 8.7 %copy-start.23 = (bf16[128,128]{1,0:T(8,128)(2,1)S(1)}, bf16[128,128]{1,0:T(8,128)(2,1)}, u32[]{:S(2)}) copy-start(bf16[128,128]{1,0:T(8,128)(2,1)} %get-tuple-element.41) | copy-start | bytes 98308
  191.8 8.7 %copy-start.24 = (bf16[128,128]{1,0:T(8,128)(2,1)S(1)}, bf16[128,128]{1,0:T(8,128)(2,1)}, u32[]{:S(2)}) copy-start(bf16[128,128]{1,0:T(8,128)(2,1)} %get-tuple-element.42) | copy-start | bytes 98308
  191.8 8.7 %copy-start.25 = (bf16[128,128]{1,0:T(8,128)(2,1)S(1)}, bf16[128,128]{1,0:T(8,128)(2,1)}, u32[]{:S(2)}) copy-start(bf16[128,128]{1,0:T(8,128)(2,1)} %get-tuple-element.43) | copy-start | bytes 98308
  211.4 4.0 copy-start.17
  214.1 9.1 %copy-start.31 = (s32[384]{0:T(512)S(1)}, s32[384]{0:T(512)}, u32[]{:S(2)}) copy-start(s32[384]{0:T(512)} %param.14) | copy-start | bytes 4612
  214.2 9.1 %copy-start.32 = (s32[16]{0:T(128)S(1)}, s32[16]{0:T(128)}, u32[]{:S(2)}) copy-start(s32[16]{0:T(128)} %param.15) | copy-start | bytes 196
  215.3 195.5 %all-reduce.7.cloned.1.call-start = ((), (), s32[]{:S(2)}) async-start(), calls=%async_computation.4 | async-start | bytes 6291456 | tf_op jit(solution)/shard_map/psum | solution.py:133
  223.3 87.8 %copy-start.29 = (s32[1024]{0:T(1024)}, s32[1024]{0:T(1024)S(1)}, u32[]{:S(2)}) copy-start(s32[1024]{0:T(1024)S(1)} %get-tuple-element.96) | copy-start | bytes 12292
  223.3 87.8 %copy-start.27 = (s32[2048]{0:T(1024)}, s32[2048]{0:T(1024)S(1)}, u32[]{:S(2)}) copy-start(s32[2048]{0:T(1024)S(1)} %iota_add_fusion) | copy-start | bytes 24580
  247.2 5.3 copy-start
  247.2 4.0 copy-start.20
  251.2 59.9 %copy-start.12 = (f32[2048,384]{0,1:T(8,128)}, f32[2048,384]{0,1:T(8,128)S(1)}, u32[]{:S(2)}) copy-start(f32[2048,384]{0,1:T(8,128)S(1)} %slice.365) | copy-start | bytes 9437188
  299.9 6.6 %copy-start.33 = (bf16[16,2048,128]{2,1,0:T(8,128)(2,1)S(1)}, bf16[16,2048,128]{2,1,0:T(8,128)(2,1)}, u32[]{:S(2)}) copy-start(bf16[16,2048,128]{2,1,0:T(8,128)(2,1)} %all-gather.10.cloned.1.call-done) | copy-start | bytes 25165828
  306.6 4.6 copy-start.50
  306.6 5.6 copy-start.13
  306.6 5.6 copy-start.19
  306.6 5.5 copy-start.34
  341.2 129.7 %all-gather.12.cloned.1.call-start = ((), (), s32[]{:S(2)}) async-start(), calls=%async_computation.6 | async-start | bytes 2949120 | tf_op jit(solution)/shard_map/all_gather | solution.py:138
  410.8 10.9 %copy-start.7 = (f32[2048,384]{1,0:T(8,128)S(1)}, f32[2048,384]{1,0:T(8,128)}, u32[]{:S(2)}) copy-start(f32[2048,384]{1,0:T(8,128)} %all-reduce.7.cloned.1.call-done) | copy-start | bytes 9437188
  420.2 183.6 %all-reduce.9.cloned.1.call-start = ((), (), s32[]{:S(2)}) async-start(), calls=%async_computation.5 | async-start | bytes 3145728 | tf_op jit(solution)/shard_map/psum | solution.py:16
  421.7 54.0 %copy-start.26 = (f32[384]{0:T(512)S(1)}, f32[384]{0:T(512)}, u32[]{:S(2)}) copy-start(f32[384]{0:T(512)} %param.17) | copy-start | bytes 4612
  594.6 9.3 %copy-start.28 = (s32[2048]{0:T(1024)S(1)}, s32[2048]{0:T(1024)}, u32[]{:S(2)}) copy-start(s32[2048]{0:T(1024)} %copy-done.27) | copy-start | bytes 24580
  594.6 9.3 %copy-start.30 = (s32[1024]{0:T(1024)S(1)}, s32[1024]{0:T(1024)}, u32[]{:S(2)}) copy-start(s32[1024]{0:T(1024)} %copy-done.29) | copy-start | bytes 12292
  594.6 9.2 %copy-start.35 = (f32[1024]{0:T(1024)S(1)}, f32[1024]{0:T(1024)}, u32[]{:S(2)}) copy-start(f32[1024]{0:T(1024)} %param.13) | copy-start | bytes 12292
  (27 other events, 49.2 us)
Sparse Core Ops, SparseCore 0:
  9.9 30.5 all-gather.5
  42.1 149.6 all-gather.7
  194.1 50.0 all-reduce.4
  246.2 53.7 all-gather.9
  341.3 69.4 all-reduce.6
  420.4 50.5 all-gather.11
  473.3 68.0 all-reduce.8
